TPU v7x, 256 devices: a whole 4x4x8 slice. The times are simulated.
256 devices in a mesh: seq: 8 (over x, core), vocab: 32 (over z, y).
Axes of the slice: x: 4, y: 4, z: 8, core: 2. Of those that a mesh axis runs over, the one named last changes fastest.
Arguments:
- hidden: bfloat16 [2048, 4096], P('seq'), may hold values from -48 to 48
- head_weight: bfloat16 [4096, 65536], P('seq', 'vocab'), may hold values from -0.09375 to 0.09375
- queries: float32 [16, 65536], P(None, 'vocab'), may hold values from 0 to 1, as said below
- passage_lengths: int32 [32], replicated, may hold values from 1 to 192, 2048 in all
- pairing: int32 [32], replicated, may hold values from 0 to 15
- doc_freq: int32 [65536], P('vocab'), may hold values from 0 to 4194304
Outputs:
- grad_hidden: bfloat16 [2048, 4096], P('seq', 'vocab')
- losses: float32 [2], replicated
Inputs may be any that keep to these rules, and one draw needn't show every extreme that they name: `queries`: entries are nonnegative.
All inputs are finite; a program needn't handle non-finite values.
Results may differ from a plain program's by a relative error of at most 0.0039.
Values may be sent and summed in bfloat16 or wider, within the bound.
No kernel may reach another device: no remote copies, remote signals or barrier semaphores. Data moves between devices by JAX's collectives and lax.ppermute only.
A program may use at most 128 MiB of HBM per device.

v0:
```python
import jax
import jax.numpy as jnp
from jax import lax
from jax.sharding import PartitionSpec as P

DOCS = 4194304
sharpness = 8.0
loss_scale = 16384.0
flops_weight = 32.0
highest = lax.Precision.HIGHEST


def softmax_terms(scores, pair_rows):
    onehot = (jnp.arange(scores.shape[0], dtype=jnp.int32)[:, None] == pair_rows[None, :]).astype(
        jnp.float32
    )
    peak_score = jnp.max(scores, axis=0)
    shifted = jnp.exp(scores - peak_score[None, :])
    denominator = jnp.sum(shifted, axis=0)
    log_total = peak_score + jnp.log(denominator)
    losses_each = log_total - jnp.sum(onehot * scores, axis=0)
    return (losses_each, shifted / denominator[None, :] - onehot)


def per_device(hidden, head_weight, queries, passage_lengths, pairing, doc_freq):
    tok_rows = hidden.shape[0]
    vocab_cols = head_weight.shape[1]
    passages = passage_lengths.shape[0]
    vocab_total = vocab_cols * lax.axis_size("vocab")
    finish = jnp.cumsum(passage_lengths)
    starts = finish - passage_lengths
    position = lax.axis_index("seq") * tok_rows + jnp.arange(tok_rows, dtype=jnp.int32)
    member = (
        (position[None, :] >= starts[:, None]) & (position[None, :] < finish[:, None])
    ).astype(jnp.float32)
    counts = passage_lengths.astype(jnp.float32)
    weights_df = jnp.log(1.0 + DOCS / (1.0 + doc_freq.astype(jnp.float32)))
    flops_grad = loss_scale * flops_weight * 2.0 / (vocab_total * passages)
    full_head = lax.all_gather(head_weight, "seq", axis=0, tiled=True)
    logits = jnp.dot(hidden, full_head, preferred_element_type=jnp.float32)
    lifted = 1.0 + jax.nn.relu(logits)
    squared = lifted * lifted
    fourth = squared * squared
    powered = fourth * fourth
    local_sums = jnp.dot(member, powered, precision=highest)
    totals = lax.psum(local_sums, "seq")
    pooled = (jnp.log(totals) - jnp.log(counts)[:, None]) / sharpness
    col_mean = jnp.sum(pooled, axis=0) / passages
    flops_part = jnp.sum(weights_df * col_mean * col_mean) / vocab_total
    scores, flops_value = lax.psum(
        (jnp.dot(queries, pooled.T, precision=highest), flops_part), "vocab"
    )
    losses_each, probs = softmax_terms(scores, pairing)
    contrast = jnp.mean(losses_each)
    dscores = probs * (loss_scale / passages)
    dpooled = jnp.dot(dscores.T, queries, precision=highest) + flops_grad * weights_df * col_mean
    factor = dpooled / totals
    spread = lax.dot_general(member, factor, (((0,), (0,)), ((), ())), precision=highest)
    seventh = fourth * squared * lifted
    dlogits = jnp.where(logits > 0, spread * seventh, 0.0).astype(jnp.bfloat16)
    grad_cols = lax.psum_scatter(
        lax.dot_general(
            full_head, dlogits, (((1,), (1,)), ((), ())), preferred_element_type=jnp.float32
        ),
        "vocab",
        scatter_dimension=0,
        tiled=True,
    )
    losses = jnp.stack([contrast, flops_value])
    return (grad_cols.T.astype(jnp.bfloat16), losses)


def solution(mesh):
    placed = (P("seq", None), P("seq", "vocab"), P(None, "vocab"), P(), P(), P("vocab"))
    return jax.shard_map(
        per_device, mesh=mesh, in_specs=placed, out_specs=(P("seq", "vocab"), P()), check_vma=False
    )
```

profile of v0, /device:TPU:2, one launch (start us, length us, event | category | flops | bytes accessed | tf_op | source)
XLA Modules:
  0.0 500.4 jit_solution(3179952712906589109)
XLA Ops:
  7.2 0.0 copy-start
  7.2 0.0 copy-start.3
  7.2 0.0 all-gather.2.cloned.1.call-start
  7.2 0.7 all-gather.2.cloned.1.call-update
  7.9 0.0 all-reduce.3.cloned.1.call-start
  8.0 0.0 copy-done.3
  8.0 0.1 copy.9
  8.1 0.1 reduce-window.8
  8.1 0.1 reduce
  8.3 91.6 %all-gather.2.cloned.1.call-done = bf16[4096,2048]{1,0:T(8,128)(2,1)} async-done(((bf16[512,2048]{1,0:T(8,128)(2,1)}), bf16[4096,2048]{1,0:T(8,128)(2,1)}) %all-gather.2.cloned.1.call-update) | async-done | bytes 16777232 | tf_op jit(solution)/shard_map/all_gather | solution.py:39
  99.9 0.0 copy-done
  99.9 8.1 %fusion.31 = f32[256,2048]{1,0:T(8,128)S(1)} fusion(bf16[256,4096]{1,0:T(8,128)(2,1)S(1)} %copy-done, bf16[4096,2048]{1,0:T(8,128)(2,1)} %all-gather.2.cloned.1.call-done), kind=kOutput, calls=%fused_computation.51 | convolution fusion | flops 4294967296 | bytes 20971520 | tf_op jit(solution)/shard_map/dot_general | solution.py:40
  108.0 0.0 copy-start.5
  108.0 1.3 copy-done.5
  109.4 1.9 fusion.3
  111.3 0.0 all-reduce.3.cloned.1.call-update
  111.3 0.0 reduce-scatter.2.cloned.1.call-start
  111.4 64.3 %all-reduce.3.cloned.1.call-done = f32[32,2048]{1,0:T(8,128)} async-done(((f32[32,2048]{1,0:T(8,128)}), f32[32,2048]{1,0:T(8,128)}) %all-reduce.3.cloned.1.call-update) | async-done | bytes 262160 | tf_op jit(solution)/shard_map/psum | solution.py:46
  175.6 1.1 fusion.8
  176.7 0.0 copy-done.2
  176.7 0.6 fusion.17
  178.0 0.0 copy-done.1
  178.0 1.3 convolution_bitcast_fusion.1
  179.3 78.1 %all-reduce = (f32[16,32]{1,0:T(8,128)S(1)}, f32[1]{0:T(128)}) all-reduce(f32[16,32]{1,0:T(8,128)S(1)} %convolution_bitcast_fusion.1, f32[1]{0:T(128)} %bitcast.5), channel_id=1, replica_groups=mesh['seq'=8,'vocab'=32] {'vocab'}, use_global_device_ids=true, to_apply=%region_2.3 | all-reduce | flops 513 | bytes 4104 | tf_op jit(solution)/shard_map/psum | solution.py:50
  257.5 1.4 fusion.2
  258.8 3.2 fusion.1
  262.0 10.1 %convolution_bitcast_fusion = f32[4096,256]{0,1:T(8,128)} fusion(bf16[256,2048]{1,0:T(8,128)(2,1)S(1)} %fusion.1, bf16[4096,2048]{1,0:T(8,128)(2,1)} %all-gather.2.cloned.1.call-done), kind=kOutput, calls=%fused_computation | convolution fusion | flops 4294967296 | bytes 22020096 | tf_op jit(solution)/shard_map/dot_general | solution.py:62
  272.1 0.0 reduce-scatter.2.cloned.1.call-update
  272.1 0.6 subtract_reduce_fusion
  273.4 1.2 pad_maximum_fusion
  274.6 217.8 %reduce-scatter.2.cloned.1.call-done = f32[128,256]{0,1:T(8,128)} async-done(((f32[4096,256]{0,1:T(8,128)}), f32[128,256]{0,1:T(8,128)}) %reduce-scatter.2.cloned.1.call-update) | async-done | bytes 131088 | tf_op jit(solution)/shard_map/reduce_scatter | solution.py:61
  492.4 1.5 convert_bitcast_fusion
  (9 shorter events, 0.1 us)
Async XLA Ops:
  7.2 92.7 %copy-start = (bf16[256,4096]{1,0:T(8,128)(2,1)S(1)}, bf16[256,4096]{1,0:T(8,128)(2,1)}, u32[]{:S(2)}) copy-start(bf16[256,4096]{1,0:T(8,128)(2,1)} %param.6) | copy-start | bytes 6291460
  7.2 0.8 copy-start.3
  7.2 92.7 %all-gather.2.cloned.1.call-start = ((), (), s32[]{:S(2)}) async-start(), calls=%async_computation.1 | async-start | bytes 18874368 | tf_op jit(solution)/shard_map/all_gather | solution.py:39
  7.9 167.7 %all-reduce.3.cloned.1.call-start = ((), (), s32[]{:S(2)}) async-start(), calls=%async_computation.2 | async-start | bytes 524288 | tf_op jit(solution)/shard_map/psum | solution.py:46
  108.0 1.4 copy-start.5
  109.4 67.3 %copy-start.2 = (s32[2048]{0:T(1024)S(1)}, s32[2048]{0:T(1024)}, u32[]{:S(2)}) copy-start(s32[2048]{0:T(1024)} %param.11) | copy-start | bytes 24580
  109.4 68.6 %copy-start.1 = (f32[16,2048]{1,0:T(8,128)S(1)}, f32[16,2048]{1,0:T(8,128)}, u32[]{:S(2)}) copy-start(f32[16,2048]{1,0:T(8,128)} %param.8) | copy-start | bytes 393220
  109.4 148.1 %copy-start.4 = (s32[32]{0:T(128)S(1)}, s32[32]{0:T(128)}, u32[]{:S(2)}) copy-start(s32[32]{0:T(128)} %param.10) | copy-start | bytes 388
  111.3 381.1 %reduce-scatter.2.cloned.1.call-start = ((), (), s32[]{:S(2)}) async-start(), calls=%async_computation.3 | async-start | bytes 4325376 | tf_op jit(solution)/shard_map/reduce_scatter | solution.py:61
Sparse Core Ops, SparseCore 0:
  9.9 89.9 all-gather.1
  111.4 64.1 all-reduce.2
  272.3 220.0 reduce-scatter.1
where the time goes:
time: 501 us; the launch traced here: 500 us
  waiting for transfers between devices  374 us (75%)
  blocking collectives  78.1 us (16%)
  matrix products  25.9 us (5%)
  between operations  15.1 us (3%)
  other arithmetic  5.3 us (1%)
    reduce_scatter x1, waiting for transfers between devices, per_device(): lax.psum_scatter(lax.dot_general(full_head, dlogits, (((1,), (1,)), ((),...  218 us
    all_gather x1, waiting for transfers between devices, per_device(): full_head = lax.all_gather(head_weight, 'seq', axis=0, tiled=True)  91.6 us
    psum x1, blocking collectives, per_device(): lax.psum((jnp.dot(queries, pooled.T, precision=highest), flops_part), 'vo...  78.1 us
    psum x1, waiting for transfers between devices, per_device(): totals = lax.psum(local_sums, 'seq')  64.3 us
    dot_general x1, matrix products, per_device(): lax.dot_general(full_head, dlogits, (((1,), (1,)), ((), ())), preferred_e...  10.1 us
  transfers between devices with their start and end apart: 3, of which 3 were waited for; matrix products, arithmetic and copies ran while one was open for 0% of the time, Pallas kernels for 0%

commit v1 on v0

--- a/solution.py
+++ b/solution.py
@@ -36,7 +36,22 @@
     counts = passage_lengths.astype(jnp.float32)
     weights_df = jnp.log(1.0 + DOCS / (1.0 + doc_freq.astype(jnp.float32)))
     flops_grad = loss_scale * flops_weight * 2.0 / (vocab_total * passages)
-    full_head = lax.all_gather(head_weight, "seq", axis=0, tiled=True)
+    ways, here, step = (lax.axis_size("seq"), lax.axis_index("seq"), head_weight.shape[0])
+    shape = [n * ways if d == 0 else n for d, n in enumerate(head_weight.shape)]
+    full_head = lax.dynamic_update_slice_in_dim(
+        jnp.zeros(shape, head_weight.dtype), head_weight, here * step, axis=0
+    )
+    going_up = going_down = head_weight
+    for far in range(1, ways // 2 + 1):
+        going_up = lax.ppermute(going_up, "seq", [(d, (d + 1) % ways) for d in range(ways)])
+        full_head = lax.dynamic_update_slice_in_dim(
+            full_head, going_up, (here - far) % ways * step, axis=0
+        )
+        if 2 * far < ways:
+            going_down = lax.ppermute(going_down, "seq", [(d, (d - 1) % ways) for d in range(ways)])
+            full_head = lax.dynamic_update_slice_in_dim(
+                full_head, going_down, (here + far) % ways * step, axis=0
+            )
     logits = jnp.dot(hidden, full_head, preferred_element_type=jnp.float32)
     lifted = 1.0 + jax.nn.relu(logits)
     squared = lifted * lifted

time: 501 us -> 516 us (1.030)
  local copies, waits for them, and re-layouts: 1.46 us -> 20.7 us
  waiting for transfers between devices: 374 us -> 368 us
    all_gather x1 -> x0, waiting for transfers between devices: 91.6 us -> none  [per_device(): full_head = lax.all_gather(head_weight, 'seq', axis=0, tiled=True)]
    ppermute x0 -> x7, waiting for transfers between devices: none -> 82.6 us  [the longest x4 82.6 us: per_device(): lax.ppermute(going_up, 'seq', [(d, (d + 1) % ways) for d in range(ways)])]
    dynamic_update_slice x0 -> x8, local copies, waits for them, and re-layouts: none -> 8.56 us  [the longest x4 4.28 us: per_device(): lax.dynamic_update_slice_in_dim(full_head, going_up, (here - far) % ways...]
    unnamed x12 -> x29, local copies, waits for them, and re-layouts: 1.38 us -> 9.32 us
  transfers between devices with their start and end apart: 3 -> 9, of which waited for: 3 -> 6; matrix products, arithmetic and copies ran while one was open for 0% -> 2% of each run, Pallas kernels for 0% -> 0%
where the time goes in v1:
time: 516 us; the launch traced here: 515 us
  waiting for transfers between devices  368 us (71%)
  blocking collectives  78.3 us (15%)
  matrix products  23 us (4%)
  local copies, waits for them, and re-layouts  20.7 us (4%)
  between operations  15.6 us (3%)
  other arithmetic  5.32 us (1%)
    reduce_scatter x1, waiting for transfers between devices, per_device(): lax.psum_scatter(lax.dot_general(full_head, dlogits, (((1,), (1,)), ((),...  217 us
    ppermute x4, waiting for transfers between devices, per_device(): lax.ppermute(going_up, 'seq', [(d, (d + 1) % ways) for d in range(ways)])  82.6 us
    psum x1, blocking collectives, per_device(): lax.psum((jnp.dot(queries, pooled.T, precision=highest), flops_part), 'vo...  78.3 us
    psum x1, waiting for transfers between devices, per_device(): totals = lax.psum(local_sums, 'seq')  68.6 us
  transfers between devices with their start and end apart: 9, of which 6 were waited for; matrix products, arithmetic and copies ran while one was open for 2% of the time, Pallas kernels for 0%

profile of v1, /device:TPU:2, one launch (start us, length us, event | category | flops | bytes accessed | tf_op | source)
XLA Modules:
  0.0 515.0 jit_solution(1638162825314162774)
XLA Ops:
  7.3 1.7 collective-permute-start.1
  9.0 23.9 %collective-permute-done = bf16[512,2048]{1,0:T(8,128)(2,1)S(1)} collective-permute-done((bf16[512,2048]{1,0:T(8,128)(2,1)}, bf16[512,2048]{1,0:T(8,128)(2,1)S(1)}, u32[]{:S(2)}, u32[]{:S(2)}) %collective-permute-start) | collective-permute-done | bytes 2097184 | tf_op jit(solution)/shard_map/ppermute | solution.py:46
  32.9 1.3 copy-done.3
  34.2 1.7 collective-permute-start.3
  36.0 23.7 %collective-permute-done.2 = bf16[512,2048]{1,0:T(8,128)(2,1)S(1)} collective-permute-done((bf16[512,2048]{1,0:T(8,128)(2,1)S(1)}, bf16[512,2048]{1,0:T(8,128)(2,1)S(1)}, u32[]{:S(2)}, u32[]{:S(2)}) %collective-permute-start.2) | collective-permute-done | bytes 2097184 | tf_op jit(solution)/shard_map/ppermute | solution.py:46
  59.7 1.3 copy-done.7
  61.0 0.8 collective-permute-start.5
  61.7 23.5 %collective-permute-done.4 = bf16[512,2048]{1,0:T(8,128)(2,1)} collective-permute-done((bf16[512,2048]{1,0:T(8,128)(2,1)S(1)}, bf16[512,2048]{1,0:T(8,128)(2,1)}, u32[]{:S(2)}, u32[]{:S(2)}) %collective-permute-start.4) | collective-permute-done | bytes 2097184 | tf_op jit(solution)/shard_map/ppermute | solution.py:46
  85.3 0.7 copy.10
  86.8 2.0 broadcast_in_dim.3
  89.2 1.3 copy-done.4
  90.8 1.3 copy-done.6
  92.4 1.3 copy-done.8
  94.0 1.9 constant_dynamic-update-slice_fusion.3
  95.8 1.9 constant_dynamic-update-slice_fusion.2
  97.7 1.9 constant_dynamic-update-slice_fusion.1
  99.6 11.4 %collective-permute-done.6 = bf16[512,2048]{1,0:T(8,128)(2,1)} collective-permute-done((bf16[512,2048]{1,0:T(8,128)(2,1)}, bf16[512,2048]{1,0:T(8,128)(2,1)}, u32[]{:S(2)}, u32[]{:S(2)}) %collective-permute-start.6) | collective-permute-done | bytes 2097184 | tf_op jit(solution)/shard_map/ppermute | solution.py:46
  111.0 1.9 constant_dynamic-update-slice_fusion
  112.9 5.1 fusion.28
  118.7 1.3 copy-done.13
  120.0 2.2 fusion.1
  122.3 68.6 %all-reduce.3.cloned.1.call-done = f32[32,2048]{1,0:T(8,128)} async-done(((f32[32,2048]{1,0:T(8,128)}), f32[32,2048]{1,0:T(8,128)}) %all-reduce.3.cloned.1.call-update) | async-done | bytes 262160 | tf_op jit(solution)/shard_map/psum | solution.py:61
  190.8 1.1 fusion.5
  193.2 1.3 convolution_bitcast_fusion
  194.5 78.3 %all-reduce = (f32[16,32]{1,0:T(8,128)S(1)}, f32[1]{0:T(128)}) all-reduce(f32[16,32]{1,0:T(8,128)S(1)} %convolution_bitcast_fusion, f32[1]{0:T(128)} %bitcast.6), channel_id=1, replica_groups=mesh['seq'=8,'vocab'=32] {'vocab'}, use_global_device_ids=true, to_apply=%region_2.3 | all-reduce | flops 513 | bytes 4104 | tf_op jit(solution)/shard_map/psum | solution.py:65
  272.9 1.4 fusion
  274.2 3.0 select_convert_fusion
  277.3 10.1 %fusion.29 = f32[4096,256]{1,0:T(8,128)} fusion(bf16[4096,2048]{1,0:T(8,128)(2,1)} %copy-done.1, bf16[256,2048]{0,1:T(8,128)(2,1)S(1)} %select_convert_fusion), kind=kOutput, calls=%fused_computation.58 | convolution fusion | flops 4294967296 | bytes 22020096 | tf_op jit(solution)/shard_map/dot_general | solution.py:77
  288.6 1.2 pad_maximum_fusion
  289.9 216.7 %reduce-scatter.2.cloned.1.call-done = f32[128,256]{1,0:T(8,128)} async-done(((f32[4096,256]{1,0:T(8,128)}), f32[128,256]{1,0:T(8,128)}) %reduce-scatter.2.cloned.1.call-update) | async-done | bytes 131088 | tf_op jit(solution)/shard_map/reduce_scatter | solution.py:76
  506.6 0.9 convert_bitcast_fusion
  507.5 0.7 copy.11
  (46 shorter events, 4.0 us)
Async XLA Ops:
  7.2 105.8 %copy-start = (bf16[256,4096]{1,0:T(8,128)(2,1)S(1)}, bf16[256,4096]{1,0:T(8,128)(2,1)}, u32[]{:S(2)}) copy-start(bf16[256,4096]{1,0:T(8,128)(2,1)} %param.6) | copy-start | bytes 6291460
  7.2 183.7 %all-reduce.3.cloned.1.call-start = ((), (), s32[]{:S(2)}) async-start(), calls=%async_computation.1 | async-start | bytes 524288 | tf_op jit(solution)/shard_map/psum | solution.py:61
  7.2 25.7 %collective-permute-start = (bf16[512,2048]{1,0:T(8,128)(2,1)}, bf16[512,2048]{1,0:T(8,128)(2,1)S(1)}, u32[]{:S(2)}, u32[]{:S(2)}) collective-permute-start(bf16[512,2048]{1,0:T(8,128)(2,1)} %param.7), channel_id=1, source_target_pairs={{0,32},{32,64},{64,96},{96,128},{128,160},{160,192},{192,224},{224... | collective-permute-start | bytes 6291464 | tf_op jit(solution)/shard_map/ppermute | solution.py:46
  7.3 27.0 %collective-permute-start.1 = (bf16[512,2048]{1,0:T(8,128)(2,1)}, bf16[512,2048]{1,0:T(8,128)(2,1)S(1)}, u32[]{:S(2)}, u32[]{:S(2)}) collective-permute-start(bf16[512,2048]{1,0:T(8,128)(2,1)} %param.7), channel_id=1, source_target_pairs={{0,224},{32,0},{64,32},{96,64},{128,96},{160,128},{192,160},{224,1... | collective-permute-start | bytes 6291464 | tf_op jit(solution)/shard_map/ppermute | solution.py:51
  32.9 1.3 copy-start.3
  34.2 25.5 %collective-permute-start.2 = (bf16[512,2048]{1,0:T(8,128)(2,1)S(1)}, bf16[512,2048]{1,0:T(8,128)(2,1)S(1)}, u32[]{:S(2)}, u32[]{:S(2)}) collective-permute-start(bf16[512,2048]{1,0:T(8,128)(2,1)S(1)} %collective-permute-done), channel_id=1, source_target_pairs={{0,32},{32,64},{64,96},{96,128},{128,160},{160,192},{192,224},{224... | collective-permute-start | bytes 6291464 | tf_op jit(solution)/shard_map/ppermute | solution.py:46
  34.2 25.5 %copy-start.5 = (bf16[512,2048]{1,0:T(8,128)(2,1)}, bf16[512,2048]{1,0:T(8,128)(2,1)S(1)}, u32[]{:S(2)}) copy-start(bf16[512,2048]{1,0:T(8,128)(2,1)S(1)} %collective-permute-done.1) | copy-start | bytes 6291460
  34.2 25.5 %collective-permute-start.3 = (bf16[512,2048]{1,0:T(8,128)(2,1)S(1)}, bf16[512,2048]{1,0:T(8,128)(2,1)}, u32[]{:S(2)}, u32[]{:S(2)}) collective-permute-start(bf16[512,2048]{1,0:T(8,128)(2,1)S(1)} %collective-permute-done.1), channel_id=1, source_target_pairs={{0,224},{32,0},{64,32},{96,64},{128,96},{160,128},{192,160},{224,1... | collective-permute-start | bytes 6291464 | tf_op jit(solution)/shard_map/ppermute | solution.py:51
  59.7 1.3 copy-start.7
  59.7 25.6 %collective-permute-start.4 = (bf16[512,2048]{1,0:T(8,128)(2,1)S(1)}, bf16[512,2048]{1,0:T(8,128)(2,1)}, u32[]{:S(2)}, u32[]{:S(2)}) collective-permute-start(bf16[512,2048]{1,0:T(8,128)(2,1)S(1)} %collective-permute-done.2), channel_id=1, source_target_pairs={{0,32},{32,64},{64,96},{96,128},{128,160},{160,192},{192,224},{224... | collective-permute-start | bytes 6291464 | tf_op jit(solution)/shard_map/ppermute | solution.py:46
  61.0 36.7 %collective-permute-start.5 = (bf16[512,2048]{1,0:T(8,128)(2,1)}, bf16[512,2048]{1,0:T(8,128)(2,1)}, u32[]{:S(2)}, u32[]{:S(2)}) collective-permute-start(bf16[512,2048]{1,0:T(8,128)(2,1)} %collective-permute-done.3), channel_id=1, source_target_pairs={{0,224},{32,0},{64,32},{96,64},{128,96},{160,128},{192,160},{224,1... | collective-permute-start | bytes 6291464 | tf_op jit(solution)/shard_map/ppermute | solution.py:51
  85.3 25.8 %collective-permute-start.6 = (bf16[512,2048]{1,0:T(8,128)(2,1)}, bf16[512,2048]{1,0:T(8,128)(2,1)}, u32[]{:S(2)}, u32[]{:S(2)}) collective-permute-start(bf16[512,2048]{1,0:T(8,128)(2,1)} %collective-permute-done.4), channel_id=1, source_target_pairs={{0,32},{32,64},{64,96},{96,128},{128,160},{160,192},{192,224},{224... | collective-permute-start | bytes 6291464 | tf_op jit(solution)/shard_map/ppermute | solution.py:46
  86.8 2.1 copy-start.2
  88.9 1.6 copy-start.4
  90.5 1.6 copy-start.6
  92.1 1.6 copy-start.8
  112.9 5.7 %copy-start.1 = (bf16[4096,2048]{1,0:T(8,128)(2,1)}, bf16[4096,2048]{1,0:T(8,128)(2,1)S(1)}, u32[]{:S(2)}) copy-start(bf16[4096,2048]{1,0:T(8,128)(2,1)S(1)} %constant_dynamic-update-slice_fusion) | copy-start | bytes 50331652
  118.7 1.4 copy-start.13
  120.0 2.2 copy-start.11
  120.0 71.9 %copy-start.10 = (s32[2048]{0:T(1024)S(1)}, s32[2048]{0:T(1024)}, u32[]{:S(2)}) copy-start(s32[2048]{0:T(1024)} %param.11) | copy-start | bytes 24580
  120.0 73.2 %copy-start.9 = (f32[16,2048]{1,0:T(8,128)S(1)}, f32[16,2048]{1,0:T(8,128)}, u32[]{:S(2)}) copy-start(f32[16,2048]{1,0:T(8,128)} %param.8) | copy-start | bytes 393220
  120.0 152.8 %copy-start.12 = (s32[32]{0:T(128)S(1)}, s32[32]{0:T(128)}, u32[]{:S(2)}) copy-start(s32[32]{0:T(128)} %param.10) | copy-start | bytes 388
  122.2 384.4 %reduce-scatter.2.cloned.1.call-start = ((), (), s32[]{:S(2)}) async-start(), calls=%async_computation.2 | async-start | bytes 4325376 | tf_op jit(solution)/shard_map/reduce_scatter | solution.py:76
Sparse Core Ops, SparseCore 0:
  122.3 68.4 all-reduce.2
  287.5 219.0 reduce-scatter.1
